TPU v7x, 256 devices: a whole 4x4x8 slice. The times are simulated.
256 devices in a mesh: expert: 32 (over x, z), tensor: 8 (over y, core).
Axes of the slice: x: 4, y: 4, z: 8, core: 2. Of those that a mesh axis runs over, the one named last changes fastest.
Arguments:
- attn_vals: bfloat16 [2048, 4096], P('expert', 'tensor'), may hold values from -6 to 6
- residual: bfloat16 [2048, 4096], P('expert', 'tensor'), may hold values from -6 to 6
- out_weight: bfloat16 [4096, 4096], P('tensor'), may hold values from -0.09375 to 0.09375
- norm_gain: float32 [4096], P('tensor'), may hold values from 0.5 to 1.5
- router_weight: float32 [4096, 8], P('tensor'), may hold values from -0.09375 to 0.09375
- routes: int32 [2048, 2], P('expert'), may hold values from 0 to 7, all different within a row; in each aligned block of 64 rows (0 to 63, 64 to 127, ...) at most 32 rows name the same one
- w_gate: bfloat16 [32, 4096, 2048], P('expert', None, 'tensor'), may hold values from -0.09375 to 0.09375
- w_up: bfloat16 [32, 4096, 2048], P('expert', None, 'tensor'), may hold values from -0.09375 to 0.09375
- w_down: bfloat16 [32, 2048, 4096], P('expert', 'tensor'), may hold values from -0.0625 to 0.0625
- slab_of: int32 [32], replicated, may hold values from 0 to 31, each once
- final_gain: float32 [4096], P('tensor'), may hold values from 0.5 to 1.5
- row_order: int32 [2048], replicated, may hold values from 0 to 2047, each once
Outputs:
- stream_out: bfloat16 [2048, 4096], P('expert', 'tensor')
- normed_out: bfloat16 [2048, 4096], P('expert', 'tensor')
Inputs may be any that keep to these rules, and one draw needn't show every extreme that they name: `routes`: the two experts of a row differ. In each aligned block of 64 rows (the rows of one device) no expert is named by more than 32 rows, and some block names one expert exactly 32 times. `slab_of`: A permutation. `row_order`: A permutation.
All inputs are finite; a program needn't handle non-finite values.
Results may differ from a plain program's by a relative error of at most 0.017.
Values may be sent and summed in bfloat16 or wider, within the bound.
No kernel may reach another device: no remote copies, remote signals or barrier semaphores. Data moves between devices by JAX's collectives and lax.ppermute only.
A program may use at most 128 MiB of HBM per device.

v0:
```python
import jax
import jax.numpy as jnp
from jax import lax
from jax.sharding import PartitionSpec as P

D = 4096
MOST = 32
EPS = 1e-05


def finish_slots(gate_val, up_val, down_weight):
    active = (jax.nn.silu(gate_val) * up_val).astype(jnp.bfloat16)
    partial_out = jnp.einsum("gmf,fd->gmd", active, down_weight, preferred_element_type=jnp.float32)
    summed = lax.psum_scatter(
        partial_out.astype(jnp.bfloat16), "tensor", scatter_dimension=2, tiled=True
    )
    return lax.all_to_all(summed, "expert", split_axis=0, concat_axis=0, tiled=True)


def final_norm(stream, final_gain):
    stream_f = stream.astype(jnp.float32)
    square_total = lax.psum(jnp.sum(stream_f * stream_f, axis=1), "tensor")
    factor = lax.rsqrt(square_total / D + EPS)
    return (stream_f * factor[:, None] * final_gain).astype(jnp.bfloat16)


def on_device(
    attn_vals,
    residual,
    out_weight,
    norm_gain,
    router_weight,
    routes,
    w_gate,
    w_up,
    w_down,
    slab_of,
    final_gain,
    row_order,
):
    groups = lax.axis_size("expert")
    row_count = attn_vals.shape[0]
    expert_count = router_weight.shape[1]
    slab_count = groups // expert_count
    partial_proj = jnp.dot(attn_vals, out_weight, preferred_element_type=jnp.float32)
    project = lax.psum_scatter(
        partial_proj.astype(jnp.bfloat16), "tensor", scatter_dimension=1, tiled=True
    ).astype(jnp.float32)
    stream_in = (residual.astype(jnp.float32) + project).astype(jnp.bfloat16)
    hidden_f = stream_in.astype(jnp.float32)
    scaled = hidden_f * norm_gain
    square_sum, logit_part = lax.psum(
        (
            jnp.sum(hidden_f * hidden_f, axis=1),
            jnp.dot(scaled, router_weight, precision=lax.Precision.HIGHEST),
        ),
        "tensor",
    )
    inverse_rms = lax.rsqrt(square_sum / D + EPS)
    normed_in = (scaled * inverse_rms[:, None]).astype(jnp.bfloat16)
    logits = logit_part * inverse_rms[:, None]
    expert_ids = jnp.arange(expert_count, dtype=jnp.int32)
    route_hot = (routes[:, :, None] == expert_ids[None, None, :]).astype(jnp.int32)
    chosen = jnp.sum(route_hot.astype(jnp.float32) * logits[:, None, :], axis=2)
    leading = jax.nn.sigmoid(chosen[:, 0] - chosen[:, 1])
    mixing = jnp.stack([leading, 1.0 - leading], axis=1)
    route_hits = jnp.sum(route_hot, axis=1)
    before_count = jnp.cumsum(route_hits, axis=0) - route_hits
    slot_ids = jnp.sum(route_hot * before_count[:, None, :], axis=2)
    slot_hot = (slot_ids[:, :, None] == jnp.arange(MOST, dtype=jnp.int32)[None, None, :]).astype(
        jnp.float32
    )
    placing = jnp.einsum("rke,rks->esr", route_hot.astype(jnp.float32), slot_hot).astype(
        jnp.bfloat16
    )
    target_expert = slab_of // slab_count
    send_map = jnp.take(placing, target_expert, axis=0)
    outgoing = jnp.einsum(
        "gsr,rd->gsd", send_map, normed_in, preferred_element_type=jnp.float32
    ).astype(jnp.bfloat16)
    arrived_part = lax.all_to_all(outgoing, "expert", split_axis=0, concat_axis=0, tiled=True)
    arrived = lax.all_gather(arrived_part, "tensor", axis=2, tiled=True)
    gate_val = jnp.einsum("gmd,df->gmf", arrived, w_gate[0], preferred_element_type=jnp.float32)
    up_val = jnp.einsum("gmd,df->gmf", arrived, w_up[0], preferred_element_type=jnp.float32)
    returned = finish_slots(gate_val, up_val, w_down[0])
    group_ids = jnp.arange(groups, dtype=jnp.int32)
    holder_hot = (slab_of[None, :] == group_ids[:, None]).astype(jnp.int32)
    holders = jnp.sum(holder_hot * group_ids[None, :], axis=1).reshape(expert_count, slab_count)
    row_holders = jnp.take(holders, routes, axis=0)
    flat_index = row_holders * MOST + slot_ids[:, :, None]
    flat_back = returned.reshape(groups * MOST, returned.shape[2])
    fetched = jnp.take(flat_back, flat_index.reshape(-1), axis=0).reshape(
        row_count, 2, slab_count, returned.shape[2]
    )
    expert_out = jnp.sum(fetched.astype(jnp.float32), axis=2)
    blended = jnp.sum(mixing[:, :, None] * expert_out, axis=1)
    stream = (hidden_f + blended).astype(jnp.bfloat16)
    positions = lax.axis_index("expert") * row_count + jnp.arange(row_count, dtype=jnp.int32)
    matches = (row_order[None, :] == positions[:, None]).astype(jnp.int32)
    source = jnp.sum(matches * jnp.arange(row_order.shape[0], dtype=jnp.int32)[None, :], axis=1)
    all_stream = lax.all_gather(stream, "expert", axis=0, tiled=True)
    ordered = jnp.take(all_stream, source, axis=0)
    return (ordered, final_norm(ordered, final_gain))


def solution(mesh):
    return jax.shard_map(
        on_device,
        mesh=mesh,
        in_specs=(
            P("expert", "tensor"),
            P("expert", "tensor"),
            P("tensor", None),
            P("tensor"),
            P("tensor", None),
            P("expert", None),
            P("expert", None, "tensor"),
            P("expert", None, "tensor"),
            P("expert", "tensor", None),
            P(),
            P("tensor"),
            P(),
        ),
        out_specs=(P("expert", "tensor"), P("expert", "tensor")),
        check_vma=False,
    )
```

profile of v0, /device:TPU:1, one launch (start us, length us, event | category | flops | bytes accessed | tf_op | source)
XLA Modules:
  0.0 367.0 jit_solution(5263027604369193061)
XLA Ops:
  7.2 4.0 %convolution_convert_fusion.1 = bf16[64,4096]{1,0:T(8,128)(2,1)} fusion(bf16[64,512]{1,0:T(8,128)(2,1)} %param.12, bf16[512,4096]{1,0:T(8,128)(2,1)} %param.14), kind=kOutput, calls=%fused_computation.5 | convolution fusion | flops 268697600 | bytes 4784128 | tf_op jit(solution)/shard_map/dot_general | solution.py:45
  11.3 0.1 copy.71
  11.4 0.2 convert_reduce_fusion.1
  11.6 0.1 reduce_window_sum.11
  11.7 1.2 select_reduce_fusion.1
  12.9 0.4 fusion.13
  13.4 0.1 copy.80
  13.6 0.6 gather_fusion.1
  14.2 32.7 %reduce-scatter.3.cloned.1.call-done = bf16[64,512]{1,0:T(8,128)(2,1)} async-done(((bf16[64,4096]{1,0:T(8,128)(2,1)}), bf16[64,512]{1,0:T(8,128)(2,1)}) %reduce-scatter.3.cloned.1.call-update) | async-done | bytes 65552 | tf_op jit(solution)/shard_map/reduce_scatter | solution.py:46
  46.8 1.0 fusion.28
  47.8 0.2 fusion.23
  48.0 14.9 %all-reduce = (f32[64]{0:T(128)S(1)}, f32[64,8]{0,1:T(8,128)S(1)}) all-reduce(f32[64]{0:T(128)S(1)} %get-tuple-element.10, f32[64,8]{0,1:T(8,128)S(1)} %fusion.23), channel_id=1, replica_groups=mesh['expert'=32,'tensor'=8] {'tensor'}, use_global_device_ids=true, to_apply=%region_4.0 | all-reduce | flops 576 | bytes 4608 | tf_op jit(solution)/shard_map/psum | solution.py:52
  62.9 0.5 convolution_convert_fusion.2
  63.4 34.6 %all_to_all.10 = bf16[32,32,512]{2,1,0:T(8,128)(2,1)} all-to-all(bf16[32,32,512]{2,1,0:T(8,128)(2,1)S(1)} %convolution_convert_fusion.2), channel_id=1, replica_groups=mesh['expert'=32,'tensor'=8] {'expert'}, dimensions={0} | all-to-all | bytes 2097152 | tf_op jit(solution)/shard_map/all_to_all | solution.py:81
  98.1 50.6 %all-gather.3.cloned.1.call-done = bf16[32,32,4096]{2,1,0:T(8,128)(2,1)} async-done(((bf16[32,32,512]{2,1,0:T(8,128)(2,1)}), bf16[32,32,4096]{2,1,0:T(8,128)(2,1)}) %all-gather.3.cloned.1.call-update) | async-done | bytes 8388624 | tf_op jit(solution)/shard_map/all_gather | solution.py:82
  148.7 6.3 %fusion.3 = f32[32,32,256]{2,1,0:T(8,128)S(1)} fusion(bf16[32,32,4096]{2,1,0:T(8,128)(2,1)} %all-gather.3.cloned.1.call-done, bf16[1,4096,256]{2,1,0:T(8,128)(2,1)} %param.18), kind=kOutput, calls=%fused_computation.9 | convolution fusion | flops 2147483648 | bytes 11534336 | tf_op jit(solution)/shard_map/gmd,df->gmf/dot_general | solution.py:83
  155.0 16.8 %convolution_convert_fusion = bf16[32,32,4096]{2,1,0:T(8,128)(2,1)} fusion(bf16[1,256,4096]{2,1,0:T(8,128)(2,1)S(1)} %copy-done, bf16[32,32,4096]{2,1,0:T(8,128)(2,1)} %all-gather.3.cloned.1.call-done, bf16[1,4096,256]{2,1,0:T(8,128)(2,1)} %param.19, f32[32,32,256]{2,1,0:T(8,128)S(1)} %fusion.3), kind=kOutput, calls=%fused_computation.4 | convolution fusion | flops 4300734464 | bytes 22020096 | tf_op jit(solution)/shard_map/gmf,fd->gmd/dot_general | solution.py:13
  171.8 54.4 %reduce-scatter.5.cloned.1.call-done = bf16[32,32,512]{2,1,0:T(8,128)(2,1)} async-done(((bf16[32,32,4096]{2,1,0:T(8,128)(2,1)}), bf16[32,32,512]{2,1,0:T(8,128)(2,1)}) %reduce-scatter.5.cloned.1.call-update) | async-done | bytes 1048592 | tf_op jit(solution)/shard_map/reduce_scatter | solution.py:14
  226.2 9.5 %all-to-all-start.1 = ((bf16[32,32,512]{2,1,0:T(8,128)(2,1)}), bf16[32,32,512]{2,1,0:T(8,128)(2,1)S(1)}, u32[]{:S(2)}, u32[]{:S(2)}) async-start(bf16[32,32,512]{2,1,0:T(8,128)(2,1)} %reduce-scatter.5.cloned.1.call-done), calls=%async_computation.3 | async-start | bytes 2097152 | tf_op jit(solution)/shard_map/all_to_all | solution.py:17
  235.8 0.2 all-gather.5.cloned.1.call-start
  236.0 0.1 copy.78
  236.1 0.1 copy.76
  236.2 0.1 reshape.129
  236.3 0.1 select_reduce_fusion.2
  236.5 0.1 reshape.125
  236.6 0.6 gather_fusion
  237.2 0.1 copy.77
  237.3 0.1 copy.81
  237.4 0.1 add.139
  237.6 0.1 copy.79
  237.8 0.1 copy.72
  237.9 0.2 fusion.33
  238.1 0.1 fusion.45
  238.2 0.1 copy.84
  238.2 0.1 copy.85
  238.4 0.1 copy.75
  238.4 22.5 %all-to-all-done.1 = bf16[32,32,512]{2,1,0:T(8,128)(2,1)S(1)} async-done(((bf16[32,32,512]{2,1,0:T(8,128)(2,1)}), bf16[32,32,512]{2,1,0:T(8,128)(2,1)S(1)}, u32[]{:S(2)}, u32[]{:S(2)}) %all-to-all-start.1) | async-done | bytes 1048608 | tf_op jit(solution)/shard_map/all_to_all | solution.py:17
  261.0 2.6 gather_fusion.2
  263.6 1.2 gather.21
  264.8 0.9 convert_reduce_fusion
  265.7 0.4 multiply_reduce_fusion
  266.1 0.6 fusion.29
  266.8 0.2 select_reduce_fusion
  267.1 72.8 %all-gather.5.cloned.1.call-done = bf16[2048,512]{1,0:T(8,128)(2,1)} async-done(((bf16[64,512]{1,0:T(8,128)(2,1)}), bf16[2048,512]{1,0:T(8,128)(2,1)}) %all-gather.5.cloned.1.call-update) | async-done | bytes 2097168 | tf_op jit(solution)/shard_map/all_gather | solution.py:101
  339.9 2.6 gather_fusion.3
  342.5 0.2 fusion.25
  342.7 17.1 %psum.23 = f32[64]{0:T(128)S(1)} all-reduce(f32[64]{0:T(128)S(1)} %get-tuple-element.4), channel_id=1, replica_groups=mesh['expert'=32,'tensor'=8] {'tensor'}, use_global_device_ids=true, to_apply=%region_14.15 | all-reduce | flops 64 | bytes 512 | tf_op jit(solution)/shard_map/psum | solution.py:22
  359.7 0.7 fusion.27
  (43 shorter events, 0.4 us)
Async XLA Ops:
  7.2 147.8 %copy-start = (bf16[1,256,4096]{2,1,0:T(8,128)(2,1)S(1)}, bf16[1,256,4096]{2,1,0:T(8,128)(2,1)}, u32[]{:S(2)}) copy-start(bf16[1,256,4096]{2,1,0:T(8,128)(2,1)} %param.20) | copy-start | bytes 6291460
  7.2 4.1 %copy-start.6 = (s32[64,2]{0,1:T(2,128)S(1)}, s32[64,2]{0,1:T(2,128)}, u32[]{:S(2)}) copy-start(s32[64,2]{0,1:T(2,128)} %param.17) | copy-start | bytes 1540
  7.2 39.6 %reduce-scatter.3.cloned.1.call-start = ((), (), s32[]{:S(2)}) async-start(), calls=%async_computation.4 | async-start | bytes 589824 | tf_op jit(solution)/shard_map/reduce_scatter | solution.py:46
  11.2 2.3 copy-start.8
  11.2 35.6 %copy-start.2 = (bf16[64,512]{1,0:T(8,128)(2,1)S(1)}, bf16[64,512]{1,0:T(8,128)(2,1)}, u32[]{:S(2)}) copy-start(bf16[64,512]{1,0:T(8,128)(2,1)} %param.13) | copy-start | bytes 196612
  11.2 36.6 %copy-start.3 = (f32[512,8]{0,1:T(8,128)S(1)}, f32[512,8]{0,1:T(8,128)}, u32[]{:S(2)}) copy-start(f32[512,8]{0,1:T(8,128)} %param.16) | copy-start | bytes 49156
  11.2 36.6 %copy-start.4 = (f32[512]{0:T(512)S(1)}, f32[512]{0:T(512)}, u32[]{:S(2)}) copy-start(f32[512]{0:T(512)} %param.15) | copy-start | bytes 6148
  11.3 137.4 %all-gather.3.cloned.1.call-start = ((), (), s32[]{:S(2)}) async-start(), calls=%async_computation.5 | async-start | bytes 9437184 | tf_op jit(solution)/shard_map/all_gather | solution.py:82
  98.0 128.2 %reduce-scatter.5.cloned.1.call-start = ((), (), s32[]{:S(2)}) async-start(), calls=%async_computation.6 | async-start | bytes 9437184 | tf_op jit(solution)/shard_map/reduce_scatter | solution.py:14
  226.2 34.7 %all-to-all-start.1 = ((bf16[32,32,512]{2,1,0:T(8,128)(2,1)}), bf16[32,32,512]{2,1,0:T(8,128)(2,1)S(1)}, u32[]{:S(2)}, u32[]{:S(2)}) async-start(bf16[32,32,512]{2,1,0:T(8,128)(2,1)} %reduce-scatter.5.cloned.1.call-done), calls=%async_computation.3 | async-start | bytes 2097152 | tf_op jit(solution)/shard_map/all_to_all | solution.py:17
  235.8 104.1 %all-gather.5.cloned.1.call-start = ((), (), s32[]{:S(2)}) async-start(), calls=%async_computation.7 | async-start | bytes 2162688 | tf_op jit(solution)/shard_map/all_gather | solution.py:101
  263.6 3.2 copy-start.5
  263.6 96.2 %copy-start.7 = (f32[512]{0:T(512)S(1)}, f32[512]{0:T(512)}, u32[]{:S(2)}) copy-start(f32[512]{0:T(512)} %param.22) | copy-start | bytes 6148
  342.6 17.8 %copy-start.1 = (bf16[64,512]{1,0:T(8,128)(2,1)}, bf16[64,512]{1,0:T(8,128)(2,1)S(1)}, u32[]{:S(2)}) copy-start(bf16[64,512]{1,0:T(8,128)(2,1)S(1)} %get-tuple-element.5) | copy-start | bytes 196612
Sparse Core Ops, SparseCore 0:
  11.4 35.4 reduce-scatter.2
  98.1 50.5 all-gather.2
  172.0 54.2 reduce-scatter.4
  266.9 72.9 all-gather.4
where the time goes:
time: 367 us
  waiting for transfers between devices  233 us (63%)
  blocking collectives  66.5 us (18%)
  matrix products  28.2 us (8%)
  between operations  14.1 us (4%)
  starting transfers between devices  9.88 us (3%)
  local copies, waits for them, and re-layouts  9.17 us (2%)
  other arithmetic  6.03 us (2%)
    all_gather x1, waiting for transfers between devices, on_device(): all_stream = lax.all_gather(stream, 'expert', axis=0, tiled=True)  72.8 us
    reduce_scatter x1, waiting for transfers between devices, finish_slots(): lax.psum_scatter(partial_out.astype(jnp.bfloat16), 'tensor', scatter_dime...  54.4 us
    all_gather x1, waiting for transfers between devices, on_device(): arrived = lax.all_gather(arrived_part, 'tensor', axis=2, tiled=True)  50.6 us
    all_to_all x1, blocking collectives, on_device(): lax.all_to_all(outgoing, 'expert', split_axis=0, concat_axis=0, tiled=True)  34.6 us
    reduce_scatter x1, waiting for transfers between devices, on_device(): lax.psum_scatter(partial_proj.astype(jnp.bfloat16), 'tensor', scatter_dim...  32.7 us
    all_to_all x1, waiting for transfers between devices, finish_slots(): lax.all_to_all(summed, 'expert', split_axis=0, concat_axis=0, tiled=True)  22.5 us
    psum x1, blocking collectives, final_norm(): square_total = lax.psum(jnp.sum(stream_f * stream_f, axis=1), 'tensor')  17.1 us
    dot_general x1, matrix products, finish_slots(): jnp.einsum('gmf,fd->gmd', active, down_weight, preferred_element_type=jnp...  16.8 us
  transfers between devices with their start and end apart: 5, of which 5 were waited for; matrix products, arithmetic and copies ran while one was open for 1% of the time, Pallas kernels for 0%

commit v1 on v0

--- a/solution.py
+++ b/solution.py
@@ -6,6 +6,12 @@
 D = 4096
 MOST = 32
 EPS = 1e-05
+
+
+def laid_out(pieces, dim):
+    pieces = jnp.moveaxis(pieces, 0, dim)
+    lengths = pieces.shape
+    return pieces.reshape(*lengths[:dim], lengths[dim] * lengths[dim + 1], *lengths[dim + 2 :])
 
 
 def finish_slots(gate_val, up_val, down_weight):
@@ -79,7 +85,19 @@
         "gsr,rd->gsd", send_map, normed_in, preferred_element_type=jnp.float32
     ).astype(jnp.bfloat16)
     arrived_part = lax.all_to_all(outgoing, "expert", split_axis=0, concat_axis=0, tiled=True)
-    arrived = lax.all_gather(arrived_part, "tensor", axis=2, tiled=True)
+    size = lax.axis_size("tensor")
+    pairs = [(i, (i + 1) % size) for i in range(size)]
+    back = [(b, a) for a, b in pairs]
+    lower, upper = ([], [])
+    for step in range(size - 1):
+        if step % 2 == 0:
+            lower.append(lax.ppermute(lower[-1] if lower else arrived_part, "tensor", pairs))
+        else:
+            upper.append(lax.ppermute(upper[-1] if upper else arrived_part, "tensor", back))
+    pieces = jnp.stack([*lower[::-1], arrived_part, *upper])
+    shift = lax.axis_index("tensor") - len(lower)
+    pieces = pieces[(jnp.arange(size) - shift) % size]
+    arrived = laid_out(pieces, 2)
     gate_val = jnp.einsum("gmd,df->gmf", arrived, w_gate[0], preferred_element_type=jnp.float32)
     up_val = jnp.einsum("gmd,df->gmf", arrived, w_up[0], preferred_element_type=jnp.float32)
     returned = finish_slots(gate_val, up_val, w_down[0])

time: 367 us -> 410 us (1.12)
  local copies, waits for them, and re-layouts: 9.17 us -> 42 us
  starting transfers between devices: 9.88 us -> 32.1 us
  waiting for transfers between devices: 233 us -> 219 us
    all_gather x1 -> x0, waiting for transfers between devices: 50.6 us -> none  [on_device(): arrived = lax.all_gather(arrived_part, 'tensor', axis=2, tiled=True)]
    ppermute x0 -> x7, waiting for transfers between devices: none -> 35.3 us  [the longest x4 34.2 us: on_device(): lax.ppermute(lower[-1] if lower else arrived_part, 'tensor', pairs)]
    ppermute x0 -> x7, starting transfers between devices: none -> 22.2 us  [the longest x3 12 us: on_device(): lax.ppermute(upper[-1] if upper else arrived_part, 'tensor', back)]
    unnamed x21 -> x28, local copies, waits for them, and re-layouts: 0.28 us -> 16 us
    reshape x0 -> x1, local copies, waits for them, and re-layouts: none -> 8.05 us  [laid_out(): pieces.reshape(*lengths[:dim], lengths[dim] * lengths[dim + 1], *lengths[...]
    gather x0 -> x1, local copies, waits for them, and re-layouts: none -> 8.04 us  [on_device(): pieces = pieces[(jnp.arange(size) - shift) % size]]
  transfers between devices with their start and end apart: 5 -> 11, of which waited for: 5 -> 10; matrix products, arithmetic and copies ran while one was open for 1% -> 5% of each run, Pallas kernels for 0% -> 0%
where the time goes in v1:
time: 410 us
  waiting for transfers between devices  219 us (53%)
  blocking collectives  66.5 us (16%)
  local copies, waits for them, and re-layouts  42 us (10%)
  starting transfers between devices  32.1 us (8%)
  matrix products  29.1 us (7%)
  between operations  14 us (3%)
  other arithmetic  6.73 us (2%)
    all_gather x1, waiting for transfers between devices, on_device(): all_stream = lax.all_gather(stream, 'expert', axis=0, tiled=True)  72.8 us
    reduce_scatter x1, waiting for transfers between devices, finish_slots(): lax.psum_scatter(partial_out.astype(jnp.bfloat16), 'tensor', scatter_dime...  57.1 us
    all_to_all x1, blocking collectives, on_device(): lax.all_to_all(outgoing, 'expert', split_axis=0, concat_axis=0, tiled=True)  34.5 us
    ppermute x4, waiting for transfers between devices, on_device(): lax.ppermute(lower[-1] if lower else arrived_part, 'tensor', pairs)  34.2 us
    reduce_scatter x1, waiting for transfers between devices, on_device(): lax.psum_scatter(partial_proj.astype(jnp.bfloat16), 'tensor', scatter_dim...  31.4 us
    all_to_all x1, waiting for transfers between devices, finish_slots(): lax.all_to_all(summed, 'expert', split_axis=0, concat_axis=0, tiled=True)  22.5 us
    psum x1, blocking collectives, final_norm(): square_total = lax.psum(jnp.sum(stream_f * stream_f, axis=1), 'tensor')  17.1 us
    dot_general x1, matrix products, finish_slots(): jnp.einsum('gmf,fd->gmd', active, down_weight, preferred_element_type=jnp...  16.8 us
  transfers between devices with their start and end apart: 11, of which 10 were waited for; matrix products, arithmetic and copies ran while one was open for 5% of the time, Pallas kernels for 0%

profile of v1, /device:TPU:1, one launch (start us, length us, event | category | flops | bytes accessed | tf_op | source)
XLA Modules:
  0.0 409.5 jit_solution(16150398641386019278)
XLA Ops:
  7.2 4.0 convolution_convert_fusion.1
  11.3 0.8 copy.78
  12.3 1.2 select_reduce_fusion.1
  13.6 0.4 fusion.13
  14.2 0.7 compare_and_fusion.1
  14.9 0.6 gather_fusion.1
  15.5 31.4 %reduce-scatter.3.cloned.1.call-done = bf16[64,512]{1,0:T(8,128)(2,1)} async-done(((bf16[64,4096]{1,0:T(8,128)(2,1)}), bf16[64,512]{1,0:T(8,128)(2,1)}) %reduce-scatter.3.cloned.1.call-update) | async-done | bytes 65552 | tf_op jit(solution)/shard_map/reduce_scatter | solution.py:52
  46.8 1.0 fusion.28
  47.8 0.9 fusion.23
  48.7 14.9 %all-reduce = (f32[64]{0:T(128)S(1)}, f32[64,8]{0,1:T(8,128)S(1)}) all-reduce(f32[64]{0:T(128)S(1)} %get-tuple-element.10, f32[64,8]{0,1:T(8,128)S(1)} %fusion.23), channel_id=1, replica_groups=mesh['expert'=32,'tensor'=8] {'tensor'}, use_global_device_ids=true, to_apply=%region_4.0 | all-reduce | flops 576 | bytes 4608 | tf_op jit(solution)/shard_map/psum | solution.py:58
  63.7 1.2 convolution_convert_fusion.2
  64.8 34.5 %all_to_all.10 = bf16[32,32,512]{2,1,0:T(8,128)(2,1)S(1)} all-to-all(bf16[32,32,512]{2,1,0:T(8,128)(2,1)S(1)} %convolution_convert_fusion.2), channel_id=1, replica_groups=mesh['expert'=32,'tensor'=8] {'expert'}, dimensions={0} | all-to-all | bytes 2097152 | tf_op jit(solution)/shard_map/all_to_all | solution.py:87
  99.3 2.7 collective-permute-start
  102.0 11.7 %collective-permute-done = bf16[32,32,512]{2,1,0:T(8,128)(2,1)S(1)} collective-permute-done((bf16[32,32,512]{2,1,0:T(8,128)(2,1)S(1)}, bf16[32,32,512]{2,1,0:T(8,128)(2,1)S(1)}, u32[]{:S(2)}, u32[]{:S(2)}) %collective-permute-start) | collective-permute-done | bytes 1048608 | tf_op jit(solution)/shard_map/ppermute | solution.py:94
  113.8 2.5 collective-permute-start.1
  116.2 3.1 collective-permute-start.4
  119.3 8.6 %collective-permute-done.1 = bf16[32,32,512]{2,1,0:T(8,128)(2,1)S(1)} collective-permute-done((bf16[32,32,512]{2,1,0:T(8,128)(2,1)S(1)}, bf16[32,32,512]{2,1,0:T(8,128)(2,1)S(1)}, u32[]{:S(2)}, u32[]{:S(2)}) %collective-permute-start.1) | collective-permute-done | bytes 1048608 | tf_op jit(solution)/shard_map/ppermute | solution.py:94
  128.0 2.5 collective-permute-start.2
  130.8 4.0 collective-permute-start.5
  134.8 7.4 %collective-permute-done.2 = bf16[32,32,512]{2,1,0:T(8,128)(2,1)} collective-permute-done((bf16[32,32,512]{2,1,0:T(8,128)(2,1)S(1)}, bf16[32,32,512]{2,1,0:T(8,128)(2,1)}, u32[]{:S(2)}, u32[]{:S(2)}) %collective-permute-start.2) | collective-permute-done | bytes 1048608 | tf_op jit(solution)/shard_map/ppermute | solution.py:94
  142.2 2.6 collective-permute-start.3
  144.8 0.8 collective-permute-done.5
  145.6 4.9 %collective-permute-start.6 = (bf16[32,32,512]{2,1,0:T(8,128)(2,1)}, bf16[32,32,512]{2,1,0:T(8,128)(2,1)S(1)}, u32[]{:S(2)}, u32[]{:S(2)}) collective-permute-start(bf16[32,32,512]{2,1,0:T(8,128)(2,1)} %collective-permute-done.5), channel_id=1, source_target_pairs={{1,0},{2,1},{3,2},{4,3},{5,4},{6,5},{7,6},{0,7},{9,8},{10,9},{11,1... | collective-permute-start | bytes 3145736 | tf_op jit(solution)/shard_map/ppermute | solution.py:96
  150.5 6.4 %collective-permute-done.3 = bf16[32,32,512]{2,1,0:T(8,128)(2,1)} collective-permute-done((bf16[32,32,512]{2,1,0:T(8,128)(2,1)}, bf16[32,32,512]{2,1,0:T(8,128)(2,1)}, u32[]{:S(2)}, u32[]{:S(2)}) %collective-permute-start.3) | collective-permute-done | bytes 1048608 | tf_op jit(solution)/shard_map/ppermute | solution.py:94
  156.8 2.3 bitcast_dynamic-update-slice_fusion.7
  159.2 2.4 bitcast_dynamic-update-slice_fusion.6
  161.5 2.3 bitcast_dynamic-update-slice_fusion.5
  163.9 2.3 bitcast_dynamic-update-slice_fusion.4
  166.2 1.1 bitcast_dynamic-update-slice_fusion.3
  167.2 2.4 bitcast_dynamic-update-slice_fusion.2
  169.6 2.3 bitcast_dynamic-update-slice_fusion.1
  171.9 1.1 bitcast_dynamic-update-slice_fusion
  173.0 8.0 %gather_fusion.2 = bf16[8,32,32,512]{3,2,1,0:T(8,128)(2,1)} fusion(bf16[8,32,32,512]{3,2,1,0:T(8,128)(2,1)} %bitcast_dynamic-update-slice_fusion, s32[1024]{0:T(1024)S(1)} %pad_clamp_fusion.2), kind=kCustom, calls=%fused_computation.2 | custom fusion | bytes 16777248 | tf_op jit(solution)/shard_map/gather | solution.py:99
  181.0 8.1 %copy.94 = bf16[8,32,4,8,512]{4,3,0,2,1:T(8,128)(2,1)} copy(bf16[8,32,4,8,512]{4,3,2,1,0:T(8,128)(2,1)} %bitcast.56) | data formatting | bytes 16777216 | tf_op jit(solution)/shard_map/reshape | solution.py:14
  189.1 5.7 %fusion.3 = f32[32,32,256]{2,1,0:T(8,128)S(1)} fusion(bf16[32,32,4096]{2,1,0:T(8,128)(2,1)} %bitcast.58, bf16[1,4096,256]{2,1,0:T(8,128)(2,1)S(1)} %copy-done.7), kind=kOutput, calls=%fused_computation.10 | convolution fusion | flops 2147483648 | bytes 11534336 | tf_op jit(solution)/shard_map/gmd,df->gmf/dot_general | solution.py:101
  194.8 16.8 %convolution_convert_fusion = bf16[32,32,4096]{2,1,0:T(8,128)(2,1)} fusion(bf16[1,256,4096]{2,1,0:T(8,128)(2,1)S(1)} %copy-done, bf16[32,32,4096]{2,1,0:T(8,128)(2,1)} %bitcast.59, bf16[1,4096,256]{2,1,0:T(8,128)(2,1)} %param.19, f32[32,32,256]{2,1,0:T(8,128)S(1)} %fusion.3), kind=kOutput, calls=%fused_computation.5 | convolution fusion | flops 4300734464 | bytes 22020096 | tf_op jit(solution)/shard_map/gmf,fd->gmd/dot_general | solution.py:19
  211.7 57.1 %reduce-scatter.5.cloned.1.call-done = bf16[32,32,512]{2,1,0:T(8,128)(2,1)} async-done(((bf16[32,32,4096]{2,1,0:T(8,128)(2,1)}), bf16[32,32,512]{2,1,0:T(8,128)(2,1)}) %reduce-scatter.5.cloned.1.call-update) | async-done | bytes 1048592 | tf_op jit(solution)/shard_map/reduce_scatter | solution.py:20
  268.8 9.5 %all-to-all-start.1 = ((bf16[32,32,512]{2,1,0:T(8,128)(2,1)}), bf16[32,32,512]{2,1,0:T(8,128)(2,1)S(1)}, u32[]{:S(2)}, u32[]{:S(2)}) async-start(bf16[32,32,512]{2,1,0:T(8,128)(2,1)} %reduce-scatter.5.cloned.1.call-done), calls=%async_computation.3 | async-start | bytes 2097152 | tf_op jit(solution)/shard_map/all_to_all | solution.py:23
  279.2 0.6 gather_fusion
  281.1 22.5 %all-to-all-done.1 = bf16[32,32,512]{2,1,0:T(8,128)(2,1)S(1)} async-done(((bf16[32,32,512]{2,1,0:T(8,128)(2,1)}), bf16[32,32,512]{2,1,0:T(8,128)(2,1)S(1)}, u32[]{:S(2)}, u32[]{:S(2)}) %all-to-all-start.1) | async-done | bytes 1048608 | tf_op jit(solution)/shard_map/all_to_all | solution.py:23
  303.5 2.6 gather_fusion.3
  306.1 1.2 gather.25
  307.3 0.9 convert_reduce_fusion
  308.6 0.6 fusion.29
  309.6 72.8 %all-gather.2.cloned.1.call-done = bf16[2048,512]{1,0:T(8,128)(2,1)} async-done(((bf16[64,512]{1,0:T(8,128)(2,1)}), bf16[2048,512]{1,0:T(8,128)(2,1)}) %all-gather.2.cloned.1.call-update) | async-done | bytes 2097168 | tf_op jit(solution)/shard_map/all_gather | solution.py:119
  382.4 2.6 gather_fusion.4
  385.2 17.1 %psum.23 = f32[64]{0:T(128)S(1)} all-reduce(f32[64]{0:T(128)S(1)} %get-tuple-element.4), channel_id=1, replica_groups=mesh['expert'=32,'tensor'=8] {'tensor'}, use_global_device_ids=true, to_apply=%region_14.15 | all-reduce | flops 64 | bytes 512 | tf_op jit(solution)/shard_map/psum | solution.py:28
  402.3 0.7 fusion.27
  (66 shorter events, 3.7 us)
Async XLA Ops:
  7.2 187.7 %copy-start = (bf16[1,256,4096]{2,1,0:T(8,128)(2,1)S(1)}, bf16[1,256,4096]{2,1,0:T(8,128)(2,1)}, u32[]{:S(2)}) copy-start(bf16[1,256,4096]{2,1,0:T(8,128)(2,1)} %param.20) | copy-start | bytes 6291460
  7.2 39.6 %reduce-scatter.3.cloned.1.call-start = ((), (), s32[]{:S(2)}) async-start(), calls=%async_computation.4 | async-start | bytes 589824 | tf_op jit(solution)/shard_map/reduce_scatter | solution.py:52
  11.2 257.6 %reduce-scatter.5.cloned.1.call-start = ((), (), s32[]{:S(2)}) async-start(), calls=%async_computation.5 | async-start | bytes 9437184 | tf_op jit(solution)/shard_map/reduce_scatter | solution.py:20
  99.3 14.4 %collective-permute-start = (bf16[32,32,512]{2,1,0:T(8,128)(2,1)S(1)}, bf16[32,32,512]{2,1,0:T(8,128)(2,1)S(1)}, u32[]{:S(2)}, u32[]{:S(2)}) collective-permute-start(bf16[32,32,512]{2,1,0:T(8,128)(2,1)S(1)} %all_to_all.10), channel_id=1, source_target_pairs={{0,1},{1,2},{2,3},{3,4},{4,5},{5,6},{6,7},{7,0},{8,9},{9,10},{10,1... | collective-permute-start | bytes 3145736 | tf_op jit(solution)/shard_map/ppermute | solution.py:94
  113.7 17.0 %copy-start.1 = (bf16[32,32,512]{2,1,0:T(8,128)(2,1)}, bf16[32,32,512]{2,1,0:T(8,128)(2,1)S(1)}, u32[]{:S(2)}) copy-start(bf16[32,32,512]{2,1,0:T(8,128)(2,1)S(1)} %collective-permute-done) | copy-start | bytes 3145732
  113.8 14.2 %collective-permute-start.1 = (bf16[32,32,512]{2,1,0:T(8,128)(2,1)S(1)}, bf16[32,32,512]{2,1,0:T(8,128)(2,1)S(1)}, u32[]{:S(2)}, u32[]{:S(2)}) collective-permute-start(bf16[32,32,512]{2,1,0:T(8,128)(2,1)S(1)} %collective-permute-done), channel_id=1, source_target_pairs={{0,1},{1,2},{2,3},{3,4},{4,5},{5,6},{6,7},{7,0},{8,9},{9,10},{10,1... | collective-permute-start | bytes 3145736 | tf_op jit(solution)/shard_map/ppermute | solution.py:94
  116.2 14.5 %collective-permute-start.4 = (bf16[32,32,512]{2,1,0:T(8,128)(2,1)S(1)}, bf16[32,32,512]{2,1,0:T(8,128)(2,1)}, u32[]{:S(2)}, u32[]{:S(2)}) collective-permute-start(bf16[32,32,512]{2,1,0:T(8,128)(2,1)S(1)} %all_to_all.10), channel_id=1, source_target_pairs={{1,0},{2,1},{3,2},{4,3},{5,4},{6,5},{7,6},{0,7},{9,8},{10,9},{11,1... | collective-permute-start | bytes 3145736 | tf_op jit(solution)/shard_map/ppermute | solution.py:96
  128.0 6.8 %copy-start.2 = (bf16[32,32,512]{2,1,0:T(8,128)(2,1)}, bf16[32,32,512]{2,1,0:T(8,128)(2,1)S(1)}, u32[]{:S(2)}) copy-start(bf16[32,32,512]{2,1,0:T(8,128)(2,1)S(1)} %collective-permute-done.1) | copy-start | bytes 3145732
  128.0 14.2 %collective-permute-start.2 = (bf16[32,32,512]{2,1,0:T(8,128)(2,1)S(1)}, bf16[32,32,512]{2,1,0:T(8,128)(2,1)}, u32[]{:S(2)}, u32[]{:S(2)}) collective-permute-start(bf16[32,32,512]{2,1,0:T(8,128)(2,1)S(1)} %collective-permute-done.1), channel_id=1, source_target_pairs={{0,1},{1,2},{2,3},{3,4},{4,5},{5,6},{6,7},{7,0},{8,9},{9,10},{10,1... | collective-permute-start | bytes 3145736 | tf_op jit(solution)/shard_map/ppermute | solution.py:94
  130.8 14.8 %collective-permute-start.5 = (bf16[32,32,512]{2,1,0:T(8,128)(2,1)}, bf16[32,32,512]{2,1,0:T(8,128)(2,1)}, u32[]{:S(2)}, u32[]{:S(2)}) collective-permute-start(bf16[32,32,512]{2,1,0:T(8,128)(2,1)} %collective-permute-done.4), channel_id=1, source_target_pairs={{1,0},{2,1},{3,2},{4,3},{5,4},{6,5},{7,6},{0,7},{9,8},{10,9},{11,1... | collective-permute-start | bytes 3145736 | tf_op jit(solution)/shard_map/ppermute | solution.py:96
  142.2 14.6 %collective-permute-start.3 = (bf16[32,32,512]{2,1,0:T(8,128)(2,1)}, bf16[32,32,512]{2,1,0:T(8,128)(2,1)}, u32[]{:S(2)}, u32[]{:S(2)}) collective-permute-start(bf16[32,32,512]{2,1,0:T(8,128)(2,1)} %collective-permute-done.2), channel_id=1, source_target_pairs={{0,1},{1,2},{2,3},{3,4},{4,5},{5,6},{6,7},{7,0},{8,9},{9,10},{10,1... | collective-permute-start | bytes 3145736 | tf_op jit(solution)/shard_map/ppermute | solution.py:94
  145.6 26.3 %collective-permute-start.6 = (bf16[32,32,512]{2,1,0:T(8,128)(2,1)}, bf16[32,32,512]{2,1,0:T(8,128)(2,1)S(1)}, u32[]{:S(2)}, u32[]{:S(2)}) collective-permute-start(bf16[32,32,512]{2,1,0:T(8,128)(2,1)} %collective-permute-done.5), channel_id=1, source_target_pairs={{1,0},{2,1},{3,2},{4,3},{5,4},{6,5},{7,6},{0,7},{9,8},{10,9},{11,1... | collective-permute-start | bytes 3145736 | tf_op jit(solution)/shard_map/ppermute | solution.py:96
  181.0 8.1 %copy-start.7 = (bf16[1,4096,256]{2,1,0:T(8,128)(2,1)S(1)}, bf16[1,4096,256]{2,1,0:T(8,128)(2,1)}, u32[]{:S(2)}) copy-start(bf16[1,4096,256]{2,1,0:T(8,128)(2,1)} %param.18) | copy-start | bytes 6291460
  211.6 67.0 %copy-start.5 = (s32[64,2]{0,1:T(2,128)S(1)}, s32[64,2]{0,1:T(2,128)}, u32[]{:S(2)}) copy-start(s32[64,2]{0,1:T(2,128)} %param.17) | copy-start | bytes 1540
  211.6 67.3 %copy-start.8 = (s32[32]{0:T(128)S(1)}, s32[32]{0:T(128)}, u32[]{:S(2)}) copy-start(s32[32]{0:T(128)} %param.21) | copy-start | bytes 388
  211.6 97.7 %copy-start.4 = (s32[2048]{0:T(1024)S(1)}, s32[2048]{0:T(1024)}, u32[]{:S(2)}) copy-start(s32[2048]{0:T(1024)} %param.23) | copy-start | bytes 24580
  211.6 190.6 %copy-start.6 = (f32[512]{0:T(512)S(1)}, f32[512]{0:T(512)}, u32[]{:S(2)}) copy-start(f32[512]{0:T(512)} %param.22) | copy-start | bytes 6148
  268.8 34.7 %all-to-all-start.1 = ((bf16[32,32,512]{2,1,0:T(8,128)(2,1)}), bf16[32,32,512]{2,1,0:T(8,128)(2,1)S(1)}, u32[]{:S(2)}, u32[]{:S(2)}) async-start(bf16[32,32,512]{2,1,0:T(8,128)(2,1)} %reduce-scatter.5.cloned.1.call-done), calls=%async_computation.3 | async-start | bytes 2097152 | tf_op jit(solution)/shard_map/all_to_all | solution.py:23
  278.4 104.0 %all-gather.2.cloned.1.call-start = ((), (), s32[]{:S(2)}) async-start(), calls=%async_computation.6 | async-start | bytes 2162688 | tf_op jit(solution)/shard_map/all_gather | solution.py:119
  385.2 17.8 %copy-start.3 = (bf16[64,512]{1,0:T(8,128)(2,1)}, bf16[64,512]{1,0:T(8,128)(2,1)S(1)}, u32[]{:S(2)}) copy-start(bf16[64,512]{1,0:T(8,128)(2,1)S(1)} %get-tuple-element.5) | copy-start | bytes 196612
Sparse Core Ops, SparseCore 0:
  11.4 35.4 reduce-scatter.2
  211.8 56.9 reduce-scatter.4
  309.4 72.9 all-gather.1
